TPU v7x, 256 devices: a whole 4x4x8 slice. The times are simulated.
256 devices in a mesh: grp: 32 (over y, z_lo, core), tp: 8 (over x, z_hi).
Axes of the slice: x: 4, y: 4, z: 8 (z_hi: 2, z_lo: 4; z = z_hi * 4 + z_lo), core: 2. Of those that a mesh axis runs over, the one named last changes fastest.
Arguments:
- tok_ids: int32 [8192], P('grp'), may hold values from 0 to 16383
- accept: int32 [8192], P('grp'), may hold values 0 or 1
- sub_ids: int32 [8192], P('grp'), may hold values from 0 to 16383
- cache_len: int32 [32], replicated, may hold values from 256 to 3840, as said below
- spill: int32 [32], replicated, may hold values from 0 to 1792, as said below
- embed: bfloat16 [16384, 2048], P('grp', 'tp'), may hold values from -6 to 6
- attn_gain: float32 [2048], replicated, may hold values from 0.25 to 1.75
- w_query: bfloat16 [2048, 2048], P(None, 'tp'), may hold values from -0.125 to 0.125
- w_key: bfloat16 [2048, 512], P(None, 'tp'), as said below
- w_value: bfloat16 [2048, 512], P(None, 'tp'), as said below
- w_out: bfloat16 [2048, 2048], P('tp'), may hold values from -2.5 to 2.5
- mlp_gain: float32 [2048], replicated, may hold values from 0.25 to 1.75
- w_gate: bfloat16 [2048, 5632], P(None, 'tp'), may hold values from -0.125 to 0.125
- w_up: bfloat16 [2048, 5632], P(None, 'tp'), may hold values from -0.125 to 0.125
- w_down: bfloat16 [5632, 2048], P('tp'), may hold values from -0.078125 to 0.078125
- cache_keys: bfloat16 [65536, 512], P('grp', 'tp'), may hold values from -320 to 320, as said below
- cache_values: bfloat16 [65536, 512], P('grp', 'tp'), may hold values from -8 to 8, as said below
Outputs:
- first_out: bfloat16 [8192, 2048], P('grp', 'tp')
- second_out: bfloat16 [8192, 2048], P('grp', 'tp')
Inputs may be any that keep to these rules, and one draw needn't show every extreme that they name: Request g keeps cache_len[g] - spill[g] >= 256 positions in slots from 0 of store g and spill[g] positions in the last slots of store (g xor 1); for every g, cache_len[g] - spill[g] + spill[g xor 1] <= 2048. Of each pair of groups 2k, 2k + 1 at most one has spill above 0. `w_key`: the 2 stored copies of a key-value head are equal. `w_value`: the 2 stored copies of a key-value head are equal. `cache_keys`: the 2 stored copies of a key-value head are equal. `cache_values`: the 2 stored copies of a key-value head are equal.
All inputs are finite; a program needn't handle non-finite values. No bound on the sum of `accept` on one device may be relied on, other than what follows from the above.
Results may differ from a plain program's by a relative error of at most 0.024.
Values may be sent and summed in bfloat16 or wider, within the bound.
No kernel may reach another device: no remote copies, remote signals or barrier semaphores. Data moves between devices by JAX's collectives and lax.ppermute only.
A program may use at most 128 MiB of HBM per device.

v0:
```python
import jax
import jax.numpy as jnp
from jax import lax
from jax.sharding import PartitionSpec as P
from jax.experimental import pallas as pl
from jax.experimental.pallas import tpu as pltpu

HD = 64
GRP = "grp"


EPSILON = 1e-05
SENTINEL = -1e30


def shifted(array, axis, step):
    n = lax.axis_size(axis)
    return lax.ppermute(array, axis, [(i, (i + step) % n) for i in range(n)])


def swapped(array, axis, bit):
    return lax.ppermute(array, axis, [(i, i ^ 1 << bit) for i in range(lax.axis_size(axis))])


def rolled(array, axis, shift):
    n = array.shape[axis]
    doubled = jnp.concatenate([array, array], axis=axis)
    return lax.dynamic_slice_in_dim(doubled, shift, n, axis)


def x_gather(pair):
    n_x = lax.axis_size("tp") // 2
    got = [pair] + [shifted(pair, "tp", 2 * k) for k in range(1, n_x)]
    return jnp.concatenate([got[-j % n_x] for j in range(n_x)], axis=1)


def tp_gather(part):
    me = lax.axis_index("tp")
    partner = swapped(part, "tp", 0)
    pair = jnp.where(
        me % 2 == 0,
        jnp.concatenate([part, partner], axis=1),
        jnp.concatenate([partner, part], axis=1),
    )
    return x_gather(pair)


def x_reduce(full):
    rows, total_width = full.shape
    n_x = lax.axis_size("tp") // 2
    span = total_width // n_x
    acc = full[:, :span].astype(jnp.float32)
    for k in range(1, n_x):
        piece = full[:, k * span : (k + 1) * span]
        acc = acc + shifted(piece, "tp", 2 * k).astype(jnp.float32)
    return acc


def tp_reduce(full):
    me = lax.axis_index("tp")
    acc = x_reduce(full)
    rows, span = acc.shape
    halves = acc.reshape(rows, 2, span // 2)
    low = me % 2 == 0
    mine = jnp.where(low, halves[:, 0], halves[:, 1])
    other = jnp.where(low, halves[:, 1], halves[:, 0])
    got = swapped(other.astype(jnp.bfloat16), "tp", 0)
    return mine + got.astype(jnp.float32)


def pair_reduce(full):
    rounded = x_reduce(full).astype(jnp.bfloat16)
    return rounded.astype(jnp.float32) + swapped(rounded, "tp", 0).astype(jnp.float32)


def rms_normed(values, gain):
    square = jnp.mean(values * values, axis=-1, keepdims=True)
    return (values * lax.rsqrt(square + EPSILON) * gain).astype(jnp.bfloat16)


def rotate(vectors, positions):
    half = vectors.shape[-1] // 2
    exponent = jnp.arange(half, dtype=jnp.float32) * (-2.0 / vectors.shape[-1])
    freqs = jnp.power(jnp.float32(10000.0), exponent)
    angles = positions.astype(jnp.float32)[:, None] * freqs[None, :]
    cosine = jnp.cos(angles)[:, None, :]
    sine = jnp.sin(angles)[:, None, :]
    first = vectors[..., :half]
    second = vectors[..., half:]
    return jnp.concatenate(
        [first * cosine - second * sine, second * cosine + first * sine], axis=-1
    )


def attention_kernel(q_ref, ko_ref, kf_ref, kn_ref, vo_ref, vf_ref, vn_ref, mo_ref, mf_ref, o_ref):
    query = q_ref[0]
    contract = (((1,), (1,)), ((), ()))
    parts = []
    for keys, mask in ((ko_ref[...], mo_ref[...]), (kf_ref[...], mf_ref[...]), (kn_ref[0], None)):
        scores = lax.dot_general(query, keys, contract, preferred_element_type=jnp.float32) * 0.125
        if mask is not None:
            scores = jnp.where(mask > 0, scores, SENTINEL)
        parts.append((scores, mask))
    top = parts[0][0].max(axis=-1, keepdims=True)
    for scores, _ in parts[1:]:
        top = jnp.maximum(top, scores.max(axis=-1, keepdims=True))
    total = jnp.zeros_like(top)
    weighted = jnp.zeros((query.shape[0], vn_ref.shape[-1]), jnp.float32)
    for (scores, mask), values in zip(parts, (vo_ref[...], vf_ref[...], vn_ref[0])):
        weights = jnp.exp(scores - top)
        if mask is not None:
            weights = jnp.where(mask > 0, weights, 0.0)
        total = total + weights.sum(axis=-1, keepdims=True)
        weighted = weighted + jnp.dot(
            weights.astype(jnp.bfloat16), values, preferred_element_type=jnp.float32
        )
    o_ref[0] = (weighted / total).astype(o_ref.dtype)


def attention(query, own_keys, far_keys, new_keys, own_values, far_values, new_values, own_mask, far_mask):
    passes, rows, depth = query.shape
    tile = 256
    n_own = own_keys.shape[0]
    n_far = far_keys.shape[0]
    n_new = new_keys.shape[1]
    n_keys = n_own + n_far + n_new
    whole = lambda shape: pl.BlockSpec(shape, lambda p, i: (0,) * len(shape))
    per_pass = pl.BlockSpec((1, n_new, depth), lambda p, i: (p, 0, 0))
    return pl.pallas_call(
        attention_kernel,
        grid=(passes, rows // tile),
        in_specs=[
            pl.BlockSpec((1, tile, depth), lambda p, i: (p, i, 0)),
            whole((n_own, depth)),
            whole((n_far, depth)),
            per_pass,
            whole((n_own, depth)),
            whole((n_far, depth)),
            per_pass,
            whole((1, n_own)),
            whole((1, n_far)),
        ],
        out_specs=pl.BlockSpec((1, tile, depth), lambda p, i: (p, i, 0)),
        out_shape=jax.ShapeDtypeStruct(query.shape, jnp.bfloat16),
        cost_estimate=pl.CostEstimate(
            flops=4 * passes * rows * n_keys * depth,
            transcendentals=passes * rows * n_keys,
            bytes_accessed=2 * (2 * passes * rows * depth + 2 * n_keys * depth),
        ),
    )(query, own_keys, far_keys, new_keys, own_values, far_values, new_values, own_mask, far_mask)


def on_device(
    tok_ids,
    accept,
    sub_ids,
    cache_len,
    spill,
    embed,
    attn_gain,
    w_query,
    w_key,
    w_value,
    w_out,
    mlp_gain,
    w_gate,
    w_up,
    w_down,
    cache_keys,
    cache_values,
):
    block = tok_ids.shape[0]
    slots = cache_keys.shape[0]
    query_local = w_query.shape[1] // HD
    stored_local = w_key.shape[1] // HD
    per_stored = query_local // stored_local
    group_index = lax.axis_index(GRP)
    own_count = cache_len[group_index] - spill[group_index]
    far_count = spill[group_index]
    positions = cache_len[group_index] + jnp.arange(block, dtype=jnp.int32)
    slot_ids = jnp.arange(slots, dtype=jnp.int32)
    tail_ids = slot_ids[block:]
    store_keys = cache_keys.reshape(slots, stored_local, HD)
    store_values = cache_values.reshape(slots, stored_local, HD)
    second_ids = jnp.where(accept == 1, sub_ids, tok_ids)

    table = lax.all_gather(embed, GRP, axis=0, tiled=True)
    both_ids = jnp.concatenate([tok_ids, second_ids])
    x_part = jnp.take(table, both_ids, axis=0)
    rows, width = x_part.shape

    tail_keys, tail_values = swapped((cache_keys[block:], cache_values[block:]), GRP, 0)
    far_keys = tail_keys.reshape(slots - block, stored_local, HD)
    far_values = tail_values.reshape(slots - block, stored_local, HD)
    far_valid = tail_ids >= slots - far_count
    own_valid = slot_ids < own_count

    own_mask = own_valid.astype(jnp.int32)[None]
    far_mask = far_valid.astype(jnp.int32)[None]
    mine_x = lax.axis_index("tp") // 2
    shift = mine_x * 2 * width
    attn_gain = rolled(attn_gain, 0, shift)
    mlp_gain = rolled(mlp_gain, 0, shift)
    w_query = rolled(w_query, 0, shift)
    w_key = rolled(w_key, 0, shift)
    w_value = rolled(w_value, 0, shift)
    w_gate = rolled(w_gate, 0, shift)
    w_up = rolled(w_up, 0, shift)
    w_out = rolled(w_out, 1, shift)
    w_down = rolled(w_down, 1, shift)

    def after(value, stage, lead):
        if lead is None:
            return value
        return lax.optimization_barrier((value, lead[stage]))[0]

    def denoise(x_part, lead=None):
        marks = {}
        x_full = tp_gather(x_part)
        marks["gathered"] = x_full
        x_full = after(x_full, "attended", lead)
        normed = rms_normed(x_full.astype(jnp.float32), attn_gain)
        query = rotate(
            jnp.dot(normed, w_query, preferred_element_type=jnp.float32).reshape(
                block, query_local, HD
            ),
            positions,
        ).astype(jnp.bfloat16)
        new_keys = rotate(
            jnp.dot(normed, w_key, preferred_element_type=jnp.float32).reshape(
                block, stored_local, HD
            ),
            positions,
        ).astype(jnp.bfloat16)
        new_values = jnp.dot(normed, w_value, preferred_element_type=jnp.float32).astype(
            jnp.bfloat16
        )
        mixed_heads = attention(
            query.reshape(1, block * per_stored, HD),
            store_keys.reshape(slots, HD),
            far_keys.reshape(slots - block, HD),
            new_keys.reshape(1, block, HD),
            store_values.reshape(slots, HD),
            far_values.reshape(slots - block, HD),
            new_values.reshape(1, block, HD),
            own_mask,
            far_mask,
        )
        mixed = mixed_heads.reshape(block, query_local * HD)
        head_term = jnp.dot(mixed, w_out, preferred_element_type=jnp.float32)
        marks["attended"] = head_term
        head_pair = pair_reduce(head_term.astype(jnp.bfloat16))
        span = head_pair.shape[1]
        x_pair = x_full[:, :span]
        resid_pair = (x_pair.astype(jnp.float32) + head_pair).astype(jnp.bfloat16)
        resid_full = x_gather(resid_pair)
        resid_part = lax.dynamic_slice_in_dim(
            resid_pair, (lax.axis_index("tp") % 2) * width, width, 1
        )
        resid_full = after(resid_full, "lifted", lead)
        normed_mlp = rms_normed(resid_full.astype(jnp.float32), mlp_gain)
        gate = jnp.dot(normed_mlp, w_gate, preferred_element_type=jnp.float32)
        lift = jnp.dot(normed_mlp, w_up, preferred_element_type=jnp.float32)
        hidden = (jax.nn.silu(gate) * lift).astype(jnp.bfloat16)
        down_term = jnp.dot(hidden, w_down, preferred_element_type=jnp.float32)
        marks["lifted"] = down_term
        down_part = tp_reduce(down_term.astype(jnp.bfloat16))
        return (resid_part.astype(jnp.float32) + down_part).astype(jnp.bfloat16), marks

    first_out, first_marks = denoise(x_part[:block])
    second_in = after(x_part[block:], "gathered", first_marks)
    second_out, _ = denoise(second_in, first_marks)
    return (first_out, second_out)


def solution(mesh):
    placed = (
        P(GRP),
        P(GRP),
        P(GRP),
        P(),
        P(),
        P(GRP, "tp"),
        P(),
        P(None, "tp"),
        P(None, "tp"),
        P(None, "tp"),
        P("tp", None),
        P(),
        P(None, "tp"),
        P(None, "tp"),
        P("tp", None),
        P(GRP, "tp"),
        P(GRP, "tp"),
    )
    return jax.shard_map(
        on_device,
        mesh=mesh,
        in_specs=placed,
        out_specs=(P(GRP, "tp"), P(GRP, "tp")),
        check_vma=False,
    )
```

profile of v0, /device:TPU:72, one launch (start us, length us, event | category | flops | bytes accessed | tf_op | source)
XLA Modules:
  0.0 297.6 jit_solution(4707739995224685060)
XLA Ops:
  14.8 65.7 %all-gather.2.cloned.1.call-done = bf16[16384,256]{1,0:T(8,128)(2,1)} async-done(((bf16[512,256]{1,0:T(8,128)(2,1)}), bf16[16384,256]{1,0:T(8,128)(2,1)}) %all-gather.2.cloned.1.call-update) | async-done | bytes 8388624 | tf_op jit(solution)/shard_map/all_gather | solution.py:187
  80.5 6.0 %gather_fusion = bf16[512,256]{1,0:T(8,128)(2,1)S(1)} fusion(bf16[16384,256]{1,0:T(8,128)(2,1)} %all-gather.2.cloned.1.call-done, s32[1024]{0:T(1024)S(1)} %pad_clamp_fusion), kind=kCustom, calls=%fused_computation | custom fusion | bytes 526336 | tf_op jit(solution)/shard_map/jit(_take)/gather | solution.py:189
  86.7 3.6 %collective-permute-start = (bf16[256,256]{1,0:T(8,128)(2,1)S(1)}, bf16[256,256]{1,0:T(8,128)(2,1)S(1)}, u32[]{:S(2)}, u32[]{:S(2)}) collective-permute-start(bf16[256,256]{1,0:T(8,128)(2,1)S(1)} %get-tuple-element.33), channel_id=1, source_target_pairs={{0,1},{1,0},{2,3},{3,2},{4,5},{5,4},{6,7},{7,6},{8,9},{9,8},{10,11... | collective-permute-start | bytes 393224 | tf_op jit(solution)/shard_map/ppermute | solution.py:22
  91.1 8.1 %collective-permute-done = bf16[256,256]{1,0:T(8,128)(2,1)S(1)} collective-permute-done((bf16[256,256]{1,0:T(8,128)(2,1)S(1)}, bf16[256,256]{1,0:T(8,128)(2,1)S(1)}, u32[]{:S(2)}, u32[]{:S(2)}) %collective-permute-start) | collective-permute-done | bytes 131104 | tf_op jit(solution)/shard_map/ppermute | solution.py:22
  100.8 2.7 collective-permute-start.2
  106.3 2.6 collective-permute-done.3
  108.9 5.8 %collective-permute-done.2 = bf16[256,512]{1,0:T(8,128)(2,1)S(1)} collective-permute-done((bf16[256,512]{1,0:T(8,128)(2,1)S(1)}, bf16[256,512]{1,0:T(8,128)(2,1)S(1)}, u32[]{:S(2)}, u32[]{:S(2)}) %collective-permute-start.2) | collective-permute-done | bytes 262176 | tf_op jit(solution)/shard_map/ppermute | solution.py:18
  115.6 2.3 fusion.73
  122.0 11.3 %shard_map.176 = bf16[1,1024,64]{2,1,0:T(8,128)(2,1)} custom-call(bf16[1,1024,64]{2,1,0:T(8,128)(2,1)} %pad_maximum_fusion.4.q_ref, bf16[2048,64]{1,0:T(8,128)(2,1)} %copy-done, bf16[1792,64]{1,0:T(8,128)(2,1)} %collective-permute-done.4.kf_ref, bf16[1,256,64]{2,1,0:T(8,128)(2,1)} %pad_maximum_fusion.6.kn_ref, bf16[2048,64]{1,0:T(8,128)(2,1)} %copy-done.1, ...), custom_call_target="tpu_custom_call" | custom-call | flops 1073741824 | bytes 1310720 | tf_op jit(solution)/shard_map/pallas_call | solution.py:129
  138.1 2.3 collective-permute-start.7
  141.9 3.6 %collective-permute-start.17 = (bf16[256,256]{1,0:T(8,128)(2,1)S(1)}, bf16[256,256]{1,0:T(8,128)(2,1)S(1)}, u32[]{:S(2)}, u32[]{:S(2)}) collective-permute-start(bf16[256,256]{1,0:T(8,128)(2,1)S(1)} %get-tuple-element.5), channel_id=1, source_target_pairs={{0,1},{1,0},{2,3},{3,2},{4,5},{5,4},{6,7},{7,6},{8,9},{9,8},{10,11... | collective-permute-start | bytes 393224 | tf_op jit(solution)/shard_map/ppermute | solution.py:22
  145.5 5.6 %collective-permute-done.17 = bf16[256,256]{1,0:T(8,128)(2,1)S(1)} collective-permute-done((bf16[256,256]{1,0:T(8,128)(2,1)S(1)}, bf16[256,256]{1,0:T(8,128)(2,1)S(1)}, u32[]{:S(2)}, u32[]{:S(2)}) %collective-permute-start.17) | collective-permute-done | bytes 131104 | tf_op jit(solution)/shard_map/ppermute | solution.py:22
  156.0 3.7 %collective-permute-start.9 = (bf16[256,512]{1,0:T(8,128)(2,1)S(1)}, bf16[256,512]{1,0:T(8,128)(2,1)S(1)}, u32[]{:S(2)}, u32[]{:S(2)}) collective-permute-start(bf16[256,512]{1,0:T(8,128)(2,1)S(1)} %add_convert_fusion.4), channel_id=1, source_target_pairs={{0,1},{1,0},{2,3},{3,2},{4,5},{5,4},{6,7},{7,6},{8,9},{9,8},{10,11... | collective-permute-start | bytes 786440 | tf_op jit(solution)/shard_map/ppermute | solution.py:22
  161.1 4.3 %collective-permute-done.19 = bf16[256,512]{1,0:T(8,128)(2,1)S(1)} collective-permute-done((bf16[256,512]{1,0:T(8,128)(2,1)S(1)}, bf16[256,512]{1,0:T(8,128)(2,1)S(1)}, u32[]{:S(2)}, u32[]{:S(2)}) %collective-permute-start.19) | collective-permute-done | bytes 262176 | tf_op jit(solution)/shard_map/ppermute | solution.py:18
  169.2 2.3 fusion.75
  174.4 11.4 %shard_map.177 = bf16[1,1024,64]{2,1,0:T(8,128)(2,1)} custom-call(bf16[1,1024,64]{2,1,0:T(8,128)(2,1)} %pad_maximum_fusion.5.q_ref, bf16[2048,64]{1,0:T(8,128)(2,1)} %copy-done, bf16[1792,64]{1,0:T(8,128)(2,1)} %collective-permute-done.4.kf_ref, bf16[1,256,64]{2,1,0:T(8,128)(2,1)} %pad_maximum_fusion.7.kn_ref, bf16[2048,64]{1,0:T(8,128)(2,1)} %copy-done.1, ...), custom_call_target="tpu_custom_call" | custom-call | flops 1073741824 | bytes 1310720 | tf_op jit(solution)/shard_map/pallas_call | solution.py:129
  193.8 2.1 collective-permute-start.11
  195.9 7.2 %collective-permute-done.21 = bf16[256,512]{1,0:T(8,128)(2,1)S(1)} collective-permute-done((bf16[256,512]{1,0:T(8,128)(2,1)S(1)}, bf16[256,512]{1,0:T(8,128)(2,1)S(1)}, u32[]{:S(2)}, u32[]{:S(2)}) %collective-permute-start.21) | collective-permute-done | bytes 262176 | tf_op jit(solution)/shard_map/ppermute | solution.py:18
  204.9 2.0 collective-permute-start.24
  208.3 6.8 %collective-permute-done.11 = bf16[256,512]{1,0:T(8,128)(2,1)S(1)} collective-permute-done((bf16[256,512]{1,0:T(8,128)(2,1)S(1)}, bf16[256,512]{1,0:T(8,128)(2,1)S(1)}, u32[]{:S(2)}, u32[]{:S(2)}) %collective-permute-start.11) | collective-permute-done | bytes 262176 | tf_op jit(solution)/shard_map/ppermute | solution.py:18
  215.4 2.7 fusion.31
  218.1 6.3 %fusion.20 = bf16[256,2048]{1,0:T(8,128)(2,1)S(1)} fusion(f32[256,704]{0,1:T(8,128)} %fusion.31, f32[2048]{0:T(1024)S(1)} %fusion.61, f32[256]{0:T(256)S(1)} %add_rsqrt_fusion.2, bf16[256,512]{1,0:T(8,128)(2,1)S(1)} %collective-permute-done.12, bf16[256,512]{1,0:T(8,128)(2,1)S(1)} %collective-permute-done.11, ...), kind=kOutput, calls=%fused_computation.65 | convolution fusion | flops 1494777856 | bytes 8595456 | tf_op jit(solution)/shard_map/dot_general | solution.py:265
  225.7 2.9 collective-permute-start.14
  232.7 2.8 collective-permute-done.13
  236.7 5.0 %collective-permute-done.14 = bf16[256,512]{1,0:T(8,128)(2,1)} collective-permute-done((bf16[256,512]{1,0:T(8,128)(2,1)}, bf16[256,512]{1,0:T(8,128)(2,1)}, u32[]{:S(2)}, u32[]{:S(2)}) %collective-permute-start.14) | collective-permute-done | bytes 262176 | tf_op jit(solution)/shard_map/ppermute | solution.py:18
  245.3 6.8 %collective-permute-done.26 = bf16[256,512]{1,0:T(8,128)(2,1)S(1)} collective-permute-done((bf16[256,512]{1,0:T(8,128)(2,1)S(1)}, bf16[256,512]{1,0:T(8,128)(2,1)S(1)}, u32[]{:S(2)}, u32[]{:S(2)}) %collective-permute-start.26) | collective-permute-done | bytes 262176 | tf_op jit(solution)/shard_map/ppermute | solution.py:18
  253.5 2.7 fusion.27
  256.2 6.3 %convolution_convert_fusion = bf16[256,2048]{1,0:T(8,128)(2,1)S(1)} fusion(f32[256,704]{0,1:T(8,128)} %fusion.27, bf16[256,2048]{1,0:T(8,128)(2,1)S(1)} %pad_maximum_fusion.3, f32[256]{0:T(256)S(1)} %add_rsqrt_fusion, f32[2048]{0:T(1024)S(1)} %fusion.61, s32[]{:T(128)S(6)} %select_n.114, bf16[2048,704]{0,1:T(8,128)(2,1)} %param.30, bf16[704,2048]{1,0:T(8,128)(2,1)} %param.31), kind=kOutput, calls=%fused_computation.18 | convolution fusion | flops 1491632128 | bytes 8595456 | tf_op jit(solution)/shard_map/dot_general | solution.py:265
  263.7 2.9 collective-permute-start.30
  269.3 3.1 %collective-permute-done.28 = bf16[256,512]{1,0:T(8,128)(2,1)S(1)} collective-permute-done((bf16[256,512]{1,0:T(8,128)(2,1)}, bf16[256,512]{1,0:T(8,128)(2,1)S(1)}, u32[]{:S(2)}, u32[]{:S(2)}) %collective-permute-start.28) | collective-permute-done | bytes 262176 | tf_op jit(solution)/shard_map/ppermute | solution.py:18
  272.4 5.0 %collective-permute-done.30 = bf16[256,512]{1,0:T(8,128)(2,1)S(1)} collective-permute-done((bf16[256,512]{1,0:T(8,128)(2,1)}, bf16[256,512]{1,0:T(8,128)(2,1)S(1)}, u32[]{:S(2)}, u32[]{:S(2)}) %collective-permute-start.30) | collective-permute-done | bytes 262176 | tf_op jit(solution)/shard_map/ppermute | solution.py:18
  282.7 7.1 %collective-permute-done.31 = bf16[256,256]{1,0:T(8,128)(2,1)S(1)} collective-permute-done((bf16[256,256]{1,0:T(8,128)(2,1)S(1)}, bf16[256,256]{1,0:T(8,128)(2,1)S(1)}, u32[]{:S(2)}, u32[]{:S(2)}) %collective-permute-start.31) | collective-permute-done | bytes 131104 | tf_op jit(solution)/shard_map/ppermute | solution.py:22
  (158 shorter events, 67.8 us)
Async XLA Ops:
  7.2 73.3 %all-gather.2.cloned.1.call-start = ((), (), s32[]{:S(2)}) async-start(), calls=%async_computation | async-start | bytes 8650752 | tf_op jit(solution)/shard_map/all_gather | solution.py:187
  9.2 112.7 %collective-permute-start.4 = (bf16[1792,64]{1,0:T(8,128)(2,1)S(1)}, bf16[1792,64]{1,0:T(8,128)(2,1)}, u32[]{:S(2)}, u32[]{:S(2)}) collective-permute-start(bf16[1792,64]{1,0:T(8,128)(2,1)S(1)} %slice.145), channel_id=1, source_target_pairs={{0,8},{8,0},{16,24},{24,16},{32,40},{40,32},{48,56},{56,48},{64,72... | collective-permute-start | bytes 688136 | tf_op jit(solution)/shard_map/ppermute | solution.py:22
  10.5 111.5 %collective-permute-start.5 = (bf16[1792,64]{1,0:T(8,128)(2,1)}, bf16[1792,64]{1,0:T(8,128)(2,1)}, u32[]{:S(2)}, u32[]{:S(2)}) collective-permute-start(bf16[1792,64]{1,0:T(8,128)(2,1)} %slice.148), channel_id=1, source_target_pairs={{0,8},{8,0},{16,24},{24,16},{32,40},{40,32},{48,56},{56,48},{64,72... | collective-permute-start | bytes 688136 | tf_op jit(solution)/shard_map/ppermute | solution.py:22
  86.7 12.4 %collective-permute-start = (bf16[256,256]{1,0:T(8,128)(2,1)S(1)}, bf16[256,256]{1,0:T(8,128)(2,1)S(1)}, u32[]{:S(2)}, u32[]{:S(2)}) collective-permute-start(bf16[256,256]{1,0:T(8,128)(2,1)S(1)} %get-tuple-element.33), channel_id=1, source_target_pairs={{0,1},{1,0},{2,3},{3,2},{4,5},{5,4},{6,7},{7,6},{8,9},{9,8},{10,11... | collective-permute-start | bytes 393224 | tf_op jit(solution)/shard_map/ppermute | solution.py:22
  99.3 9.6 %collective-permute-start.3 = (bf16[256,512]{1,0:T(8,128)(2,1)S(1)}, bf16[256,512]{1,0:T(8,128)(2,1)S(1)}, u32[]{:S(2)}, u32[]{:S(2)}) collective-permute-start(bf16[256,512]{1,0:T(8,128)(2,1)S(1)} %maximum_select_fusion), channel_id=1, source_target_pairs={{0,2},{1,3},{2,4},{3,5},{4,6},{5,7},{6,0},{7,1},{8,10},{9,11},{10,... | collective-permute-start | bytes 786440 | tf_op jit(solution)/shard_map/ppermute | solution.py:18
  100.8 13.9 %collective-permute-start.2 = (bf16[256,512]{1,0:T(8,128)(2,1)S(1)}, bf16[256,512]{1,0:T(8,128)(2,1)S(1)}, u32[]{:S(2)}, u32[]{:S(2)}) collective-permute-start(bf16[256,512]{1,0:T(8,128)(2,1)S(1)} %maximum_select_fusion), channel_id=1, source_target_pairs={{0,4},{1,5},{2,6},{3,7},{4,0},{5,1},{6,2},{7,3},{8,12},{9,13},{10,... | collective-permute-start | bytes 786440 | tf_op jit(solution)/shard_map/ppermute | solution.py:18
  103.5 11.2 %collective-permute-start.1 = (bf16[256,512]{1,0:T(8,128)(2,1)S(1)}, bf16[256,512]{1,0:T(8,128)(2,1)S(1)}, u32[]{:S(2)}, u32[]{:S(2)}) collective-permute-start(bf16[256,512]{1,0:T(8,128)(2,1)S(1)} %maximum_select_fusion), channel_id=1, source_target_pairs={{0,6},{1,7},{2,0},{3,1},{4,2},{5,3},{6,4},{7,5},{8,14},{9,15},{10,... | collective-permute-start | bytes 786440 | tf_op jit(solution)/shard_map/ppermute | solution.py:18
  136.5 17.7 %collective-permute-start.6 = (bf16[256,512]{1,0:T(8,128)(2,1)S(1)}, bf16[256,512]{1,0:T(8,128)(2,1)S(1)}, u32[]{:S(2)}, u32[]{:S(2)}) collective-permute-start(bf16[256,512]{1,0:T(8,128)(2,1)S(1)} %get-tuple-element.23), channel_id=1, source_target_pairs={{0,2},{1,3},{2,4},{3,5},{4,6},{5,7},{6,0},{7,1},{8,10},{9,11},{10,... | collective-permute-start | bytes 786440 | tf_op jit(solution)/shard_map/ppermute | solution.py:18
  138.1 17.8 %collective-permute-start.7 = (bf16[256,512]{1,0:T(8,128)(2,1)S(1)}, bf16[256,512]{1,0:T(8,128)(2,1)S(1)}, u32[]{:S(2)}, u32[]{:S(2)}) collective-permute-start(bf16[256,512]{1,0:T(8,128)(2,1)S(1)} %get-tuple-element.24), channel_id=1, source_target_pairs={{0,4},{1,5},{2,6},{3,7},{4,0},{5,1},{6,2},{7,3},{8,12},{9,13},{10,... | collective-permute-start | bytes 786440 | tf_op jit(solution)/shard_map/ppermute | solution.py:18
  140.4 15.5 %collective-permute-start.8 = (bf16[256,512]{1,0:T(8,128)(2,1)S(1)}, bf16[256,512]{1,0:T(8,128)(2,1)S(1)}, u32[]{:S(2)}, u32[]{:S(2)}) collective-permute-start(bf16[256,512]{1,0:T(8,128)(2,1)S(1)} %get-tuple-element.25), channel_id=1, source_target_pairs={{0,6},{1,7},{2,0},{3,1},{4,2},{5,3},{6,4},{7,5},{8,14},{9,15},{10,... | collective-permute-start | bytes 786440 | tf_op jit(solution)/shard_map/ppermute | solution.py:18
  141.9 9.2 %collective-permute-start.17 = (bf16[256,256]{1,0:T(8,128)(2,1)S(1)}, bf16[256,256]{1,0:T(8,128)(2,1)S(1)}, u32[]{:S(2)}, u32[]{:S(2)}) collective-permute-start(bf16[256,256]{1,0:T(8,128)(2,1)S(1)} %get-tuple-element.5), channel_id=1, source_target_pairs={{0,1},{1,0},{2,3},{3,2},{4,5},{5,4},{6,7},{7,6},{8,9},{9,8},{10,11... | collective-permute-start | bytes 393224 | tf_op jit(solution)/shard_map/ppermute | solution.py:22
  151.3 9.9 %collective-permute-start.20 = (bf16[256,512]{1,0:T(8,128)(2,1)S(1)}, bf16[256,512]{1,0:T(8,128)(2,1)S(1)}, u32[]{:S(2)}, u32[]{:S(2)}) collective-permute-start(bf16[256,512]{1,0:T(8,128)(2,1)S(1)} %maximum_select_fusion.1), channel_id=1, source_target_pairs={{0,2},{1,3},{2,4},{3,5},{4,6},{5,7},{6,0},{7,1},{8,10},{9,11},{10,... | collective-permute-start | bytes 786440 | tf_op jit(solution)/shard_map/ppermute | solution.py:18
  152.7 12.7 %collective-permute-start.19 = (bf16[256,512]{1,0:T(8,128)(2,1)S(1)}, bf16[256,512]{1,0:T(8,128)(2,1)S(1)}, u32[]{:S(2)}, u32[]{:S(2)}) collective-permute-start(bf16[256,512]{1,0:T(8,128)(2,1)S(1)} %maximum_select_fusion.1), channel_id=1, source_target_pairs={{0,4},{1,5},{2,6},{3,7},{4,0},{5,1},{6,2},{7,3},{8,12},{9,13},{10,... | collective-permute-start | bytes 786440 | tf_op jit(solution)/shard_map/ppermute | solution.py:18
  154.2 12.2 %collective-permute-start.18 = (bf16[256,512]{1,0:T(8,128)(2,1)S(1)}, bf16[256,512]{1,0:T(8,128)(2,1)S(1)}, u32[]{:S(2)}, u32[]{:S(2)}) collective-permute-start(bf16[256,512]{1,0:T(8,128)(2,1)S(1)} %maximum_select_fusion.1), channel_id=1, source_target_pairs={{0,6},{1,7},{2,0},{3,1},{4,2},{5,3},{6,4},{7,5},{8,14},{9,15},{10,... | collective-permute-start | bytes 786440 | tf_op jit(solution)/shard_map/ppermute | solution.py:18
  156.0 36.0 %collective-permute-start.9 = (bf16[256,512]{1,0:T(8,128)(2,1)S(1)}, bf16[256,512]{1,0:T(8,128)(2,1)S(1)}, u32[]{:S(2)}, u32[]{:S(2)}) collective-permute-start(bf16[256,512]{1,0:T(8,128)(2,1)S(1)} %add_convert_fusion.4), channel_id=1, source_target_pairs={{0,1},{1,0},{2,3},{3,2},{4,5},{5,4},{6,7},{7,6},{8,9},{9,8},{10,11... | collective-permute-start | bytes 786440 | tf_op jit(solution)/shard_map/ppermute | solution.py:22
  187.8 15.3 %collective-permute-start.21 = (bf16[256,512]{1,0:T(8,128)(2,1)S(1)}, bf16[256,512]{1,0:T(8,128)(2,1)S(1)}, u32[]{:S(2)}, u32[]{:S(2)}) collective-permute-start(bf16[256,512]{1,0:T(8,128)(2,1)S(1)} %get-tuple-element.17), channel_id=1, source_target_pairs={{0,2},{1,3},{2,4},{3,5},{4,6},{5,7},{6,0},{7,1},{8,10},{9,11},{10,... | collective-permute-start | bytes 786440 | tf_op jit(solution)/shard_map/ppermute | solution.py:18
  189.4 13.8 %collective-permute-start.23 = (bf16[256,512]{1,0:T(8,128)(2,1)S(1)}, bf16[256,512]{1,0:T(8,128)(2,1)S(1)}, u32[]{:S(2)}, u32[]{:S(2)}) collective-permute-start(bf16[256,512]{1,0:T(8,128)(2,1)S(1)} %get-tuple-element.18), channel_id=1, source_target_pairs={{0,6},{1,7},{2,0},{3,1},{4,2},{5,3},{6,4},{7,5},{8,14},{9,15},{10,... | collective-permute-start | bytes 786440 | tf_op jit(solution)/shard_map/ppermute | solution.py:18
  191.1 13.7 %collective-permute-start.22 = (bf16[256,512]{1,0:T(8,128)(2,1)S(1)}, bf16[256,512]{1,0:T(8,128)(2,1)S(1)}, u32[]{:S(2)}, u32[]{:S(2)}) collective-permute-start(bf16[256,512]{1,0:T(8,128)(2,1)S(1)} %get-tuple-element.19), channel_id=1, source_target_pairs={{0,4},{1,5},{2,6},{3,7},{4,0},{5,1},{6,2},{7,3},{8,12},{9,13},{10,... | collective-permute-start | bytes 786440 | tf_op jit(solution)/shard_map/ppermute | solution.py:18
  192.2 16.1 %collective-permute-start.12 = (bf16[256,512]{1,0:T(8,128)(2,1)S(1)}, bf16[256,512]{1,0:T(8,128)(2,1)S(1)}, u32[]{:S(2)}, u32[]{:S(2)}) collective-permute-start(bf16[256,512]{1,0:T(8,128)(2,1)S(1)} %add_convert_fusion.3), channel_id=1, source_target_pairs={{0,2},{1,3},{2,4},{3,5},{4,6},{5,7},{6,0},{7,1},{8,10},{9,11},{10,... | collective-permute-start | bytes 786440 | tf_op jit(solution)/shard_map/ppermute | solution.py:18
  193.8 21.3 %collective-permute-start.11 = (bf16[256,512]{1,0:T(8,128)(2,1)S(1)}, bf16[256,512]{1,0:T(8,128)(2,1)S(1)}, u32[]{:S(2)}, u32[]{:S(2)}) collective-permute-start(bf16[256,512]{1,0:T(8,128)(2,1)S(1)} %add_convert_fusion.3), channel_id=1, source_target_pairs={{0,4},{1,5},{2,6},{3,7},{4,0},{5,1},{6,2},{7,3},{8,12},{9,13},{10,... | collective-permute-start | bytes 786440 | tf_op jit(solution)/shard_map/ppermute | solution.py:18
  203.1 12.0 %collective-permute-start.10 = (bf16[256,512]{1,0:T(8,128)(2,1)S(1)}, bf16[256,512]{1,0:T(8,128)(2,1)S(1)}, u32[]{:S(2)}, u32[]{:S(2)}) collective-permute-start(bf16[256,512]{1,0:T(8,128)(2,1)S(1)} %add_convert_fusion.3), channel_id=1, source_target_pairs={{0,6},{1,7},{2,0},{3,1},{4,2},{5,3},{6,4},{7,5},{8,14},{9,15},{10,... | collective-permute-start | bytes 786440 | tf_op jit(solution)/shard_map/ppermute | solution.py:18
  204.9 24.7 %collective-permute-start.24 = (bf16[256,512]{1,0:T(8,128)(2,1)S(1)}, bf16[256,512]{1,0:T(8,128)(2,1)}, u32[]{:S(2)}, u32[]{:S(2)}) collective-permute-start(bf16[256,512]{1,0:T(8,128)(2,1)S(1)} %add_convert_fusion.1), channel_id=1, source_target_pairs={{0,1},{1,0},{2,3},{3,2},{4,5},{5,4},{6,7},{7,6},{8,9},{9,8},{10,11... | collective-permute-start | bytes 786440 | tf_op jit(solution)/shard_map/ppermute | solution.py:22
  225.3 10.2 %collective-permute-start.13 = (bf16[256,512]{1,0:T(8,128)(2,1)}, bf16[256,512]{1,0:T(8,128)(2,1)S(1)}, u32[]{:S(2)}, u32[]{:S(2)}) collective-permute-start(bf16[256,512]{1,0:T(8,128)(2,1)} %get-tuple-element.20), channel_id=1, source_target_pairs={{0,2},{1,3},{2,4},{3,5},{4,6},{5,7},{6,0},{7,1},{8,10},{9,11},{10,... | collective-permute-start | bytes 786440 | tf_op jit(solution)/shard_map/ppermute | solution.py:18
  225.7 16.0 %collective-permute-start.14 = (bf16[256,512]{1,0:T(8,128)(2,1)}, bf16[256,512]{1,0:T(8,128)(2,1)}, u32[]{:S(2)}, u32[]{:S(2)}) collective-permute-start(bf16[256,512]{1,0:T(8,128)(2,1)} %get-tuple-element.21), channel_id=1, source_target_pairs={{0,4},{1,5},{2,6},{3,7},{4,0},{5,1},{6,2},{7,3},{8,12},{9,13},{10,... | collective-permute-start | bytes 786440 | tf_op jit(solution)/shard_map/ppermute | solution.py:18
  228.6 14.0 %collective-permute-start.15 = (bf16[256,512]{1,0:T(8,128)(2,1)S(1)}, bf16[256,512]{1,0:T(8,128)(2,1)}, u32[]{:S(2)}, u32[]{:S(2)}) collective-permute-start(bf16[256,512]{1,0:T(8,128)(2,1)S(1)} %get-tuple-element.22), channel_id=1, source_target_pairs={{0,6},{1,7},{2,0},{3,1},{4,2},{5,3},{6,4},{7,5},{8,14},{9,15},{10,... | collective-permute-start | bytes 786440 | tf_op jit(solution)/shard_map/ppermute | solution.py:18
  230.7 14.6 %collective-permute-start.27 = (bf16[256,512]{1,0:T(8,128)(2,1)S(1)}, bf16[256,512]{1,0:T(8,128)(2,1)S(1)}, u32[]{:S(2)}, u32[]{:S(2)}) collective-permute-start(bf16[256,512]{1,0:T(8,128)(2,1)S(1)} %add_convert_fusion), channel_id=1, source_target_pairs={{0,2},{1,3},{2,4},{3,5},{4,6},{5,7},{6,0},{7,1},{8,10},{9,11},{10,... | collective-permute-start | bytes 786440 | tf_op jit(solution)/shard_map/ppermute | solution.py:18
  231.8 20.3 %collective-permute-start.26 = (bf16[256,512]{1,0:T(8,128)(2,1)S(1)}, bf16[256,512]{1,0:T(8,128)(2,1)S(1)}, u32[]{:S(2)}, u32[]{:S(2)}) collective-permute-start(bf16[256,512]{1,0:T(8,128)(2,1)S(1)} %add_convert_fusion), channel_id=1, source_target_pairs={{0,4},{1,5},{2,6},{3,7},{4,0},{5,1},{6,2},{7,3},{8,12},{9,13},{10,... | collective-permute-start | bytes 786440 | tf_op jit(solution)/shard_map/ppermute | solution.py:18
  235.5 16.6 %collective-permute-start.25 = (bf16[256,512]{1,0:T(8,128)(2,1)S(1)}, bf16[256,512]{1,0:T(8,128)(2,1)}, u32[]{:S(2)}, u32[]{:S(2)}) collective-permute-start(bf16[256,512]{1,0:T(8,128)(2,1)S(1)} %add_convert_fusion), channel_id=1, source_target_pairs={{0,6},{1,7},{2,0},{3,1},{4,2},{5,3},{6,4},{7,5},{8,14},{9,15},{10,... | collective-permute-start | bytes 786440 | tf_op jit(solution)/shard_map/ppermute | solution.py:18
  263.4 9.0 %collective-permute-start.28 = (bf16[256,512]{1,0:T(8,128)(2,1)}, bf16[256,512]{1,0:T(8,128)(2,1)S(1)}, u32[]{:S(2)}, u32[]{:S(2)}) collective-permute-start(bf16[256,512]{1,0:T(8,128)(2,1)} %get-tuple-element.14), channel_id=1, source_target_pairs={{0,2},{1,3},{2,4},{3,5},{4,6},{5,7},{6,0},{7,1},{8,10},{9,11},{10,... | collective-permute-start | bytes 786440 | tf_op jit(solution)/shard_map/ppermute | solution.py:18
  263.7 13.7 %collective-permute-start.30 = (bf16[256,512]{1,0:T(8,128)(2,1)}, bf16[256,512]{1,0:T(8,128)(2,1)S(1)}, u32[]{:S(2)}, u32[]{:S(2)}) collective-permute-start(bf16[256,512]{1,0:T(8,128)(2,1)} %get-tuple-element.15), channel_id=1, source_target_pairs={{0,6},{1,7},{2,0},{3,1},{4,2},{5,3},{6,4},{7,5},{8,14},{9,15},{10,... | collective-permute-start | bytes 786440 | tf_op jit(solution)/shard_map/ppermute | solution.py:18
  266.6 12.6 %collective-permute-start.29 = (bf16[256,512]{1,0:T(8,128)(2,1)S(1)}, bf16[256,512]{1,0:T(8,128)(2,1)}, u32[]{:S(2)}, u32[]{:S(2)}) collective-permute-start(bf16[256,512]{1,0:T(8,128)(2,1)S(1)} %get-tuple-element.16), channel_id=1, source_target_pairs={{0,4},{1,5},{2,6},{3,7},{4,0},{5,1},{6,2},{7,3},{8,12},{9,13},{10,... | collective-permute-start | bytes 786440 | tf_op jit(solution)/shard_map/ppermute | solution.py:18
  268.1 13.9 %collective-permute-start.16 = (bf16[256,256]{1,0:T(8,128)(2,1)}, bf16[256,256]{1,0:T(8,128)(2,1)S(1)}, u32[]{:S(2)}, u32[]{:S(2)}) collective-permute-start(bf16[256,256]{1,0:T(8,128)(2,1)} %fusion.55), channel_id=1, source_target_pairs={{0,1},{1,0},{2,3},{3,2},{4,5},{5,4},{6,7},{7,6},{8,9},{9,8},{10,11... | collective-permute-start | bytes 393224 | tf_op jit(solution)/shard_map/ppermute | solution.py:22
  (20 other events, 399.0 us)
Sparse Core Ops, SparseCore 0:
  9.9 70.5 all-gather.1
where the time goes:
time: 303 us; the launch traced here: 298 us
  waiting for transfers between devices  146 us (48%)
  starting transfers between devices  50.9 us (17%)
  matrix products  28.6 us (9%)
  Pallas kernels  22.7 us (7%)
  local copies, waits for them, and re-layouts  17.1 us (6%)
  between operations  16.9 us (6%)
  other arithmetic  15.4 us (5%)
    all_gather x1, waiting for transfers between devices, on_device(): table = lax.all_gather(embed, GRP, axis=0, tiled=True)  65.7 us
    ppermute x24, waiting for transfers between devices, shifted(): return lax.ppermute(array, axis, [(i, (i + step) % n) for i in range(n)])  58.8 us
    ppermute x24, starting transfers between devices, shifted(): return lax.ppermute(array, axis, [(i, (i + step) % n) for i in range(n)])  35.1 us
    pallas_call x2, Pallas kernels, attention(): pl.pallas_call(attention_kernel, grid=(passes, rows // tile), in_specs=[p...  22.7 us
    ppermute x8, waiting for transfers between devices, swapped(): lax.ppermute(array, axis, [(i, i ^ 1 << bit) for i in range(lax.axis_size...  20.9 us
    ppermute x8, starting transfers between devices, swapped(): lax.ppermute(array, axis, [(i, i ^ 1 << bit) for i in range(lax.axis_size...  15.8 us
    dot_general x2, matrix products, denoise(): down_term = jnp.dot(hidden, w_down, preferred_element_type=jnp.float32)  12.7 us
  transfers between devices with their start and end apart: 33, of which 21 were waited for; matrix products, arithmetic and copies ran while one was open for 15% of the time, Pallas kernels for 4%

commit v1 on v0

--- a/solution.py
+++ b/solution.py
@@ -96,20 +96,18 @@
     query = q_ref[0]
     contract = (((1,), (1,)), ((), ()))
     parts = []
-    for keys, mask in ((ko_ref[...], mo_ref[...]), (kf_ref[...], mf_ref[...]), (kn_ref[0], None)):
-        scores = lax.dot_general(query, keys, contract, preferred_element_type=jnp.float32) * 0.125
-        if mask is not None:
-            scores = jnp.where(mask > 0, scores, SENTINEL)
-        parts.append((scores, mask))
-    top = parts[0][0].max(axis=-1, keepdims=True)
-    for scores, _ in parts[1:]:
+    for keys, bias in ((ko_ref[...], mo_ref[...]), (kf_ref[...], mf_ref[...]), (kn_ref[0], None)):
+        scores = lax.dot_general(query, keys, contract, preferred_element_type=jnp.float32)
+        if bias is not None:
+            scores = scores + bias
+        parts.append(scores)
+    top = parts[0].max(axis=-1, keepdims=True)
+    for scores in parts[1:]:
         top = jnp.maximum(top, scores.max(axis=-1, keepdims=True))
     total = jnp.zeros_like(top)
     weighted = jnp.zeros((query.shape[0], vn_ref.shape[-1]), jnp.float32)
-    for (scores, mask), values in zip(parts, (vo_ref[...], vf_ref[...], vn_ref[0])):
+    for scores, values in zip(parts, (vo_ref[...], vf_ref[...], vn_ref[0])):
         weights = jnp.exp(scores - top)
-        if mask is not None:
-            weights = jnp.where(mask > 0, weights, 0.0)
         total = total + weights.sum(axis=-1, keepdims=True)
         weighted = weighted + jnp.dot(
             weights.astype(jnp.bfloat16), values, preferred_element_type=jnp.float32
@@ -185,18 +183,18 @@
     second_ids = jnp.where(accept == 1, sub_ids, tok_ids)
 
     table = lax.all_gather(embed, GRP, axis=0, tiled=True)
-    both_ids = jnp.concatenate([tok_ids, second_ids])
-    x_part = jnp.take(table, both_ids, axis=0)
-    rows, width = x_part.shape
-
-    tail_keys, tail_values = swapped((cache_keys[block:], cache_values[block:]), GRP, 0)
+    first_part = jnp.take(table, tok_ids, axis=0)
+    rows, width = first_part.shape
+
+    tails = swapped(jnp.concatenate([cache_keys[block:], cache_values[block:]], axis=1), GRP, 0)
+    tail_keys, tail_values = jnp.split(tails, 2, axis=1)
     far_keys = tail_keys.reshape(slots - block, stored_local, HD)
     far_values = tail_values.reshape(slots - block, stored_local, HD)
     far_valid = tail_ids >= slots - far_count
     own_valid = slot_ids < own_count
 
-    own_mask = own_valid.astype(jnp.int32)[None]
-    far_mask = far_valid.astype(jnp.int32)[None]
+    own_mask = jnp.where(own_valid, 0.0, SENTINEL)[None]
+    far_mask = jnp.where(far_valid, 0.0, SENTINEL)[None]
     mine_x = lax.axis_index("tp") // 2
     shift = mine_x * 2 * width
     attn_gain = rolled(attn_gain, 0, shift)
@@ -220,11 +218,14 @@
         marks["gathered"] = x_full
         x_full = after(x_full, "attended", lead)
         normed = rms_normed(x_full.astype(jnp.float32), attn_gain)
-        query = rotate(
-            jnp.dot(normed, w_query, preferred_element_type=jnp.float32).reshape(
-                block, query_local, HD
-            ),
-            positions,
+        query = (
+            rotate(
+                jnp.dot(normed, w_query, preferred_element_type=jnp.float32).reshape(
+                    block, query_local, HD
+                ),
+                positions,
+            )
+            * 0.125
         ).astype(jnp.bfloat16)
         new_keys = rotate(
             jnp.dot(normed, w_key, preferred_element_type=jnp.float32).reshape(
@@ -267,8 +268,8 @@
         down_part = tp_reduce(down_term.astype(jnp.bfloat16))
         return (resid_part.astype(jnp.float32) + down_part).astype(jnp.bfloat16), marks
 
-    first_out, first_marks = denoise(x_part[:block])
-    second_in = after(x_part[block:], "gathered", first_marks)
+    first_out, first_marks = denoise(first_part)
+    second_in = after(jnp.take(table, second_ids, axis=0), "gathered", first_marks)
     second_out, _ = denoise(second_in, first_marks)
     return (first_out, second_out)
 

time: 303 us -> 301 us (level)
  waiting for transfers between devices: 146 us -> 140 us
  local copies, waits for them, and re-layouts: 17.1 us -> 22.4 us
    ppermute x24, waiting for transfers between devices: 58.8 us -> 53.1 us  [shifted(): return lax.ppermute(array, axis, [(i, (i + step) % n) for i in range(n)])]
    gather x1 -> x2, local copies, waits for them, and re-layouts: 6.02 us -> 10.9 us  [the longest x1 5.47 us: on_device(): jnp.take(table, second_ids, axis=0)]
    ppermute x8 -> x7, starting transfers between devices: 15.8 us -> 15.6 us  [swapped(): lax.ppermute(array, axis, [(i, i ^ 1 << bit) for i in range(lax.axis_size...]
    ppermute x8 -> x7, waiting for transfers between devices: 20.9 us -> 20.9 us  [swapped(): lax.ppermute(array, axis, [(i, i ^ 1 << bit) for i in range(lax.axis_size...]
  transfers between devices with their start and end apart: 33 -> 32, of which waited for: 21 -> 20; matrix products, arithmetic and copies ran while one was open for 15% -> 15% of each run, Pallas kernels for 4% -> 4%
where the time goes in v1:
time: 301 us; the launch traced here: 295 us
  waiting for transfers between devices  140 us (47%)
  starting transfers between devices  51 us (17%)
  matrix products  27.4 us (9%)
  local copies, waits for them, and re-layouts  22.4 us (7%)
  Pallas kernels  21.8 us (7%)
  between operations  16.9 us (6%)
  other arithmetic  15.9 us (5%)
    all_gather x1, waiting for transfers between devices, on_device(): table = lax.all_gather(embed, GRP, axis=0, tiled=True)  65.3 us
    ppermute x24, waiting for transfers between devices, shifted(): return lax.ppermute(array, axis, [(i, (i + step) % n) for i in range(n)])  53.1 us
    ppermute x24, starting transfers between devices, shifted(): return lax.ppermute(array, axis, [(i, (i + step) % n) for i in range(n)])  35.3 us
    pallas_call x2, Pallas kernels, attention(): pl.pallas_call(attention_kernel, grid=(passes, rows // tile), in_specs=[p...  21.8 us
    ppermute x7, waiting for transfers between devices, swapped(): lax.ppermute(array, axis, [(i, i ^ 1 << bit) for i in range(lax.axis_size...  20.9 us
    ppermute x7, starting transfers between devices, swapped(): lax.ppermute(array, axis, [(i, i ^ 1 << bit) for i in range(lax.axis_size...  15.6 us
    dot_general x2, matrix products, denoise(): down_term = jnp.dot(hidden, w_down, preferred_element_type=jnp.float32)  12.7 us
  transfers between devices with their start and end apart: 32, of which 20 were waited for; matrix products, arithmetic and copies ran while one was open for 15% of the time, Pallas kernels for 4%

profile of v1, /device:TPU:72, one launch (start us, length us, event | category | flops | bytes accessed | tf_op | source)
XLA Modules:
  0.0 295.3 jit_solution(14033002526561852622)
XLA Ops:
  15.1 65.3 %all-gather.2.cloned.1.call-done = bf16[16384,256]{1,0:T(8,128)(2,1)} async-done(((bf16[512,256]{1,0:T(8,128)(2,1)}), bf16[16384,256]{1,0:T(8,128)(2,1)}) %all-gather.2.cloned.1.call-update) | async-done | bytes 8388624 | tf_op jit(solution)/shard_map/all_gather | solution.py:185
  80.4 5.4 %gather_fusion = bf16[256,256]{1,0:T(8,128)(2,1)S(1)} fusion(bf16[16384,256]{1,0:T(8,128)(2,1)} %all-gather.2.cloned.1.call-done, s32[1024]{0:T(1024)S(1)} %pad_clamp_fusion.1), kind=kCustom, calls=%fused_computation.clone | custom fusion | bytes 263168 | tf_op jit(solution)/shard_map/jit(_take)/gather | solution.py:186
  86.0 3.6 %collective-permute-start = (bf16[256,256]{1,0:T(8,128)(2,1)S(1)}, bf16[256,256]{1,0:T(8,128)(2,1)S(1)}, u32[]{:S(2)}, u32[]{:S(2)}) collective-permute-start(bf16[256,256]{1,0:T(8,128)(2,1)S(1)} %broadcast_select_fusion.1), channel_id=1, source_target_pairs={{0,1},{1,0},{2,3},{3,2},{4,5},{5,4},{6,7},{7,6},{8,9},{9,8},{10,11... | collective-permute-start | bytes 393224 | tf_op jit(solution)/shard_map/ppermute | solution.py:22
  90.3 8.1 %collective-permute-done = bf16[256,256]{1,0:T(8,128)(2,1)S(1)} collective-permute-done((bf16[256,256]{1,0:T(8,128)(2,1)S(1)}, bf16[256,256]{1,0:T(8,128)(2,1)S(1)}, u32[]{:S(2)}, u32[]{:S(2)}) %collective-permute-start) | collective-permute-done | bytes 131104 | tf_op jit(solution)/shard_map/ppermute | solution.py:22
  100.1 2.7 collective-permute-start.2
  105.5 5.5 %gather_fusion.1 = bf16[256,256]{1,0:T(8,128)(2,1)S(1)} fusion(bf16[16384,256]{1,0:T(8,128)(2,1)} %all-gather.2.cloned.1.call-done, s32[1024]{0:T(1024)S(1)} %pad_clamp_fusion), kind=kCustom, calls=%fused_computation.1.clone | custom fusion | bytes 263168 | tf_op jit(solution)/shard_map/jit(_take)/gather | solution.py:272
  111.0 3.0 %collective-permute-done.2 = bf16[256,512]{1,0:T(8,128)(2,1)S(1)} collective-permute-done((bf16[256,512]{1,0:T(8,128)(2,1)S(1)}, bf16[256,512]{1,0:T(8,128)(2,1)S(1)}, u32[]{:S(2)}, u32[]{:S(2)}) %collective-permute-start.2) | collective-permute-done | bytes 262176 | tf_op jit(solution)/shard_map/ppermute | solution.py:18
  116.7 2.3 fusion.75
  122.0 10.9 %shard_map.176 = bf16[1,1024,64]{2,1,0:T(8,128)(2,1)} custom-call(bf16[1,1024,64]{2,1,0:T(8,128)(2,1)} %fusion.20.q_ref, bf16[2048,64]{1,0:T(8,128)(2,1)} %copy-done, bf16[1792,64]{1,0:T(8,128)(2,1)} %get-tuple-element.34.kf_ref, bf16[1,256,64]{2,1,0:T(8,128)(2,1)} %pad_maximum_fusion.5.kn_ref, bf16[2048,64]{1,0:T(8,128)(2,1)} %copy-done.1, ...), custom_call_target="tpu_custom_call" | custom-call | flops 1073741824 | bytes 1310720 | tf_op jit(solution)/shard_map/pallas_call | solution.py:127
  136.5 2.2 collective-permute-start.6
  140.4 4.1 %collective-permute-start.16 = (bf16[256,256]{1,0:T(8,128)(2,1)S(1)}, bf16[256,256]{1,0:T(8,128)(2,1)S(1)}, u32[]{:S(2)}, u32[]{:S(2)}) collective-permute-start(bf16[256,256]{1,0:T(8,128)(2,1)S(1)} %broadcast_select_fusion), channel_id=1, source_target_pairs={{0,1},{1,0},{2,3},{3,2},{4,5},{5,4},{6,7},{7,6},{8,9},{9,8},{10,11... | collective-permute-start | bytes 393224 | tf_op jit(solution)/shard_map/ppermute | solution.py:22
  144.5 5.7 %collective-permute-done.16 = bf16[256,256]{1,0:T(8,128)(2,1)S(1)} collective-permute-done((bf16[256,256]{1,0:T(8,128)(2,1)S(1)}, bf16[256,256]{1,0:T(8,128)(2,1)S(1)}, u32[]{:S(2)}, u32[]{:S(2)}) %collective-permute-start.16) | collective-permute-done | bytes 131104 | tf_op jit(solution)/shard_map/ppermute | solution.py:22
  154.6 3.7 %collective-permute-start.8 = (bf16[256,512]{1,0:T(8,128)(2,1)S(1)}, bf16[256,512]{1,0:T(8,128)(2,1)S(1)}, u32[]{:S(2)}, u32[]{:S(2)}) collective-permute-start(bf16[256,512]{1,0:T(8,128)(2,1)S(1)} %add_convert_fusion.3), channel_id=1, source_target_pairs={{0,1},{1,0},{2,3},{3,2},{4,5},{5,4},{6,7},{7,6},{8,9},{9,8},{10,11... | collective-permute-start | bytes 786440 | tf_op jit(solution)/shard_map/ppermute | solution.py:22
  160.2 4.3 %collective-permute-done.18 = bf16[256,512]{1,0:T(8,128)(2,1)S(1)} collective-permute-done((bf16[256,512]{1,0:T(8,128)(2,1)S(1)}, bf16[256,512]{1,0:T(8,128)(2,1)S(1)}, u32[]{:S(2)}, u32[]{:S(2)}) %collective-permute-start.18) | collective-permute-done | bytes 262176 | tf_op jit(solution)/shard_map/ppermute | solution.py:18
  167.2 2.3 fusion.77
  172.5 10.9 %shard_map.177 = bf16[1,1024,64]{2,1,0:T(8,128)(2,1)} custom-call(bf16[1,1024,64]{2,1,0:T(8,128)(2,1)} %fusion.21.q_ref, bf16[2048,64]{1,0:T(8,128)(2,1)} %copy-done, bf16[1792,64]{1,0:T(8,128)(2,1)} %get-tuple-element.34.kf_ref, bf16[1,256,64]{2,1,0:T(8,128)(2,1)} %pad_maximum_fusion.6.kn_ref, bf16[2048,64]{1,0:T(8,128)(2,1)} %copy-done.1, ...), custom_call_target="tpu_custom_call" | custom-call | flops 1073741824 | bytes 1310720 | tf_op jit(solution)/shard_map/pallas_call | solution.py:127
  186.9 2.0 collective-permute-start.22
  191.3 2.1 collective-permute-start.10
  193.4 7.3 %collective-permute-done.20 = bf16[256,512]{1,0:T(8,128)(2,1)S(1)} collective-permute-done((bf16[256,512]{1,0:T(8,128)(2,1)S(1)}, bf16[256,512]{1,0:T(8,128)(2,1)S(1)}, u32[]{:S(2)}, u32[]{:S(2)}) %collective-permute-start.20) | collective-permute-done | bytes 262176 | tf_op jit(solution)/shard_map/ppermute | solution.py:18
  205.8 6.8 %collective-permute-done.10 = bf16[256,512]{1,0:T(8,128)(2,1)S(1)} collective-permute-done((bf16[256,512]{1,0:T(8,128)(2,1)S(1)}, bf16[256,512]{1,0:T(8,128)(2,1)S(1)}, u32[]{:S(2)}, u32[]{:S(2)}) %collective-permute-start.10) | collective-permute-done | bytes 262176 | tf_op jit(solution)/shard_map/ppermute | solution.py:18
  213.0 2.7 fusion.33
  215.7 6.3 %fusion.22 = bf16[256,2048]{1,0:T(8,128)(2,1)S(1)} fusion(f32[256,704]{0,1:T(8,128)} %fusion.33, f32[2048]{0:T(1024)S(1)} %fusion.63, f32[256]{0:T(256)S(1)} %add_rsqrt_fusion.2, bf16[256,512]{1,0:T(8,128)(2,1)S(1)} %collective-permute-done.11, bf16[256,512]{1,0:T(8,128)(2,1)S(1)} %collective-permute-done.10, ...), kind=kOutput, calls=%fused_computation.71 | convolution fusion | flops 1494777856 | bytes 8595456 | tf_op jit(solution)/shard_map/dot_general | solution.py:266
  223.4 3.0 %collective-permute-start.13 = (bf16[256,512]{1,0:T(8,128)(2,1)}, bf16[256,512]{1,0:T(8,128)(2,1)}, u32[]{:S(2)}, u32[]{:S(2)}) collective-permute-start(bf16[256,512]{1,0:T(8,128)(2,1)} %get-tuple-element.24), channel_id=1, source_target_pairs={{0,4},{1,5},{2,6},{3,7},{4,0},{5,1},{6,2},{7,3},{8,12},{9,13},{10,... | collective-permute-start | bytes 786440 | tf_op jit(solution)/shard_map/ppermute | solution.py:18
  230.5 1.9 collective-permute-done.12
  234.3 5.2 %collective-permute-done.13 = bf16[256,512]{1,0:T(8,128)(2,1)} collective-permute-done((bf16[256,512]{1,0:T(8,128)(2,1)}, bf16[256,512]{1,0:T(8,128)(2,1)}, u32[]{:S(2)}, u32[]{:S(2)}) %collective-permute-start.13) | collective-permute-done | bytes 262176 | tf_op jit(solution)/shard_map/ppermute | solution.py:18
  242.9 6.8 %collective-permute-done.25 = bf16[256,512]{1,0:T(8,128)(2,1)S(1)} collective-permute-done((bf16[256,512]{1,0:T(8,128)(2,1)S(1)}, bf16[256,512]{1,0:T(8,128)(2,1)S(1)}, u32[]{:S(2)}, u32[]{:S(2)}) %collective-permute-start.25) | collective-permute-done | bytes 262176 | tf_op jit(solution)/shard_map/ppermute | solution.py:18
  251.2 2.7 fusion.29
  253.9 6.3 %convolution_convert_fusion = bf16[256,2048]{1,0:T(8,128)(2,1)S(1)} fusion(f32[256,704]{0,1:T(8,128)} %fusion.29, bf16[256,2048]{1,0:T(8,128)(2,1)S(1)} %pad_maximum_fusion.3, f32[256]{0:T(256)S(1)} %add_rsqrt_fusion, f32[2048]{0:T(1024)S(1)} %fusion.63, s32[]{:T(128)S(6)} %select_n.111, bf16[2048,704]{0,1:T(8,128)(2,1)} %param.32, bf16[704,2048]{1,0:T(8,128)(2,1)} %param.33), kind=kOutput, calls=%fused_computation.19 | convolution fusion | flops 1491632128 | bytes 8595456 | tf_op jit(solution)/shard_map/dot_general | solution.py:266
  261.5 2.8 collective-permute-start.29
  267.0 3.0 %collective-permute-done.27 = bf16[256,512]{1,0:T(8,128)(2,1)S(1)} collective-permute-done((bf16[256,512]{1,0:T(8,128)(2,1)}, bf16[256,512]{1,0:T(8,128)(2,1)S(1)}, u32[]{:S(2)}, u32[]{:S(2)}) %collective-permute-start.27) | collective-permute-done | bytes 262176 | tf_op jit(solution)/shard_map/ppermute | solution.py:18
  270.0 5.0 %collective-permute-done.29 = bf16[256,512]{1,0:T(8,128)(2,1)S(1)} collective-permute-done((bf16[256,512]{1,0:T(8,128)(2,1)}, bf16[256,512]{1,0:T(8,128)(2,1)S(1)}, u32[]{:S(2)}, u32[]{:S(2)}) %collective-permute-start.29) | collective-permute-done | bytes 262176 | tf_op jit(solution)/shard_map/ppermute | solution.py:18
  280.4 7.1 %collective-permute-done.30 = bf16[256,256]{1,0:T(8,128)(2,1)S(1)} collective-permute-done((bf16[256,256]{1,0:T(8,128)(2,1)S(1)}, bf16[256,256]{1,0:T(8,128)(2,1)S(1)}, u32[]{:S(2)}, u32[]{:S(2)}) %collective-permute-start.30) | collective-permute-done | bytes 131104 | tf_op jit(solution)/shard_map/ppermute | solution.py:22
  (163 shorter events, 67.3 us)
Async XLA Ops:
  7.2 73.3 %all-gather.2.cloned.1.call-start = ((), (), s32[]{:S(2)}) async-start(), calls=%async_computation | async-start | bytes 8650752 | tf_op jit(solution)/shard_map/all_gather | solution.py:185
  9.9 94.4 %collective-permute-start.4 = (bf16[1792,128]{1,0:T(8,128)(2,1)S(1)}, bf16[1792,128]{1,0:T(8,128)(2,1)S(1)}, u32[]{:S(2)}, u32[]{:S(2)}) collective-permute-start(bf16[1792,128]{1,0:T(8,128)(2,1)S(1)} %pad_maximum_fusion.4), channel_id=1, source_target_pairs={{0,8},{8,0},{16,24},{24,16},{32,40},{40,32},{48,56},{56,48},{64,72... | collective-permute-start | bytes 1376264 | tf_op jit(solution)/shard_map/ppermute | solution.py:22
  86.0 12.4 %collective-permute-start = (bf16[256,256]{1,0:T(8,128)(2,1)S(1)}, bf16[256,256]{1,0:T(8,128)(2,1)S(1)}, u32[]{:S(2)}, u32[]{:S(2)}) collective-permute-start(bf16[256,256]{1,0:T(8,128)(2,1)S(1)} %broadcast_select_fusion.1), channel_id=1, source_target_pairs={{0,1},{1,0},{2,3},{3,2},{4,5},{5,4},{6,7},{7,6},{8,9},{9,8},{10,11... | collective-permute-start | bytes 393224 | tf_op jit(solution)/shard_map/ppermute | solution.py:22
  98.6 12.4 %collective-permute-start.3 = (bf16[256,512]{1,0:T(8,128)(2,1)S(1)}, bf16[256,512]{1,0:T(8,128)(2,1)S(1)}, u32[]{:S(2)}, u32[]{:S(2)}) collective-permute-start(bf16[256,512]{1,0:T(8,128)(2,1)S(1)} %maximum_select_fusion), channel_id=1, source_target_pairs={{0,2},{1,3},{2,4},{3,5},{4,6},{5,7},{6,0},{7,1},{8,10},{9,11},{10,... | collective-permute-start | bytes 786440 | tf_op jit(solution)/shard_map/ppermute | solution.py:18
  100.1 13.9 %collective-permute-start.2 = (bf16[256,512]{1,0:T(8,128)(2,1)S(1)}, bf16[256,512]{1,0:T(8,128)(2,1)S(1)}, u32[]{:S(2)}, u32[]{:S(2)}) collective-permute-start(bf16[256,512]{1,0:T(8,128)(2,1)S(1)} %maximum_select_fusion), channel_id=1, source_target_pairs={{0,4},{1,5},{2,6},{3,7},{4,0},{5,1},{6,2},{7,3},{8,12},{9,13},{10,... | collective-permute-start | bytes 786440 | tf_op jit(solution)/shard_map/ppermute | solution.py:18
  102.8 11.2 %collective-permute-start.1 = (bf16[256,512]{1,0:T(8,128)(2,1)S(1)}, bf16[256,512]{1,0:T(8,128)(2,1)S(1)}, u32[]{:S(2)}, u32[]{:S(2)}) collective-permute-start(bf16[256,512]{1,0:T(8,128)(2,1)S(1)} %maximum_select_fusion), channel_id=1, source_target_pairs={{0,6},{1,7},{2,0},{3,1},{4,2},{5,3},{6,4},{7,5},{8,14},{9,15},{10,... | collective-permute-start | bytes 786440 | tf_op jit(solution)/shard_map/ppermute | solution.py:18
  134.9 18.0 %collective-permute-start.5 = (bf16[256,512]{1,0:T(8,128)(2,1)S(1)}, bf16[256,512]{1,0:T(8,128)(2,1)S(1)}, u32[]{:S(2)}, u32[]{:S(2)}) collective-permute-start(bf16[256,512]{1,0:T(8,128)(2,1)S(1)} %get-tuple-element.26), channel_id=1, source_target_pairs={{0,2},{1,3},{2,4},{3,5},{4,6},{5,7},{6,0},{7,1},{8,10},{9,11},{10,... | collective-permute-start | bytes 786440 | tf_op jit(solution)/shard_map/ppermute | solution.py:18
  136.5 17.9 %collective-permute-start.6 = (bf16[256,512]{1,0:T(8,128)(2,1)S(1)}, bf16[256,512]{1,0:T(8,128)(2,1)S(1)}, u32[]{:S(2)}, u32[]{:S(2)}) collective-permute-start(bf16[256,512]{1,0:T(8,128)(2,1)S(1)} %get-tuple-element.27), channel_id=1, source_target_pairs={{0,4},{1,5},{2,6},{3,7},{4,0},{5,1},{6,2},{7,3},{8,12},{9,13},{10,... | collective-permute-start | bytes 786440 | tf_op jit(solution)/shard_map/ppermute | solution.py:18
  138.8 15.7 %collective-permute-start.7 = (bf16[256,512]{1,0:T(8,128)(2,1)S(1)}, bf16[256,512]{1,0:T(8,128)(2,1)S(1)}, u32[]{:S(2)}, u32[]{:S(2)}) collective-permute-start(bf16[256,512]{1,0:T(8,128)(2,1)S(1)} %get-tuple-element.28), channel_id=1, source_target_pairs={{0,6},{1,7},{2,0},{3,1},{4,2},{5,3},{6,4},{7,5},{8,14},{9,15},{10,... | collective-permute-start | bytes 786440 | tf_op jit(solution)/shard_map/ppermute | solution.py:18
  140.4 9.8 %collective-permute-start.16 = (bf16[256,256]{1,0:T(8,128)(2,1)S(1)}, bf16[256,256]{1,0:T(8,128)(2,1)S(1)}, u32[]{:S(2)}, u32[]{:S(2)}) collective-permute-start(bf16[256,256]{1,0:T(8,128)(2,1)S(1)} %broadcast_select_fusion), channel_id=1, source_target_pairs={{0,1},{1,0},{2,3},{3,2},{4,5},{5,4},{6,7},{7,6},{8,9},{9,8},{10,11... | collective-permute-start | bytes 393224 | tf_op jit(solution)/shard_map/ppermute | solution.py:22
  150.3 9.9 %collective-permute-start.19 = (bf16[256,512]{1,0:T(8,128)(2,1)S(1)}, bf16[256,512]{1,0:T(8,128)(2,1)S(1)}, u32[]{:S(2)}, u32[]{:S(2)}) collective-permute-start(bf16[256,512]{1,0:T(8,128)(2,1)S(1)} %maximum_select_fusion.1), channel_id=1, source_target_pairs={{0,2},{1,3},{2,4},{3,5},{4,6},{5,7},{6,0},{7,1},{8,10},{9,11},{10,... | collective-permute-start | bytes 786440 | tf_op jit(solution)/shard_map/ppermute | solution.py:18
  151.7 12.7 %collective-permute-start.18 = (bf16[256,512]{1,0:T(8,128)(2,1)S(1)}, bf16[256,512]{1,0:T(8,128)(2,1)S(1)}, u32[]{:S(2)}, u32[]{:S(2)}) collective-permute-start(bf16[256,512]{1,0:T(8,128)(2,1)S(1)} %maximum_select_fusion.1), channel_id=1, source_target_pairs={{0,4},{1,5},{2,6},{3,7},{4,0},{5,1},{6,2},{7,3},{8,12},{9,13},{10,... | collective-permute-start | bytes 786440 | tf_op jit(solution)/shard_map/ppermute | solution.py:18
  152.9 12.2 %collective-permute-start.17 = (bf16[256,512]{1,0:T(8,128)(2,1)S(1)}, bf16[256,512]{1,0:T(8,128)(2,1)S(1)}, u32[]{:S(2)}, u32[]{:S(2)}) collective-permute-start(bf16[256,512]{1,0:T(8,128)(2,1)S(1)} %maximum_select_fusion.1), channel_id=1, source_target_pairs={{0,6},{1,7},{2,0},{3,1},{4,2},{5,3},{6,4},{7,5},{8,14},{9,15},{10,... | collective-permute-start | bytes 786440 | tf_op jit(solution)/shard_map/ppermute | solution.py:18
  154.6 35.2 %collective-permute-start.8 = (bf16[256,512]{1,0:T(8,128)(2,1)S(1)}, bf16[256,512]{1,0:T(8,128)(2,1)S(1)}, u32[]{:S(2)}, u32[]{:S(2)}) collective-permute-start(bf16[256,512]{1,0:T(8,128)(2,1)S(1)} %add_convert_fusion.3), channel_id=1, source_target_pairs={{0,1},{1,0},{2,3},{3,2},{4,5},{5,4},{6,7},{7,6},{8,9},{9,8},{10,11... | collective-permute-start | bytes 786440 | tf_op jit(solution)/shard_map/ppermute | solution.py:22
  185.4 15.3 %collective-permute-start.20 = (bf16[256,512]{1,0:T(8,128)(2,1)S(1)}, bf16[256,512]{1,0:T(8,128)(2,1)S(1)}, u32[]{:S(2)}, u32[]{:S(2)}) collective-permute-start(bf16[256,512]{1,0:T(8,128)(2,1)S(1)} %get-tuple-element.20), channel_id=1, source_target_pairs={{0,2},{1,3},{2,4},{3,5},{4,6},{5,7},{6,0},{7,1},{8,10},{9,11},{10,... | collective-permute-start | bytes 786440 | tf_op jit(solution)/shard_map/ppermute | solution.py:18
  186.9 13.9 %collective-permute-start.22 = (bf16[256,512]{1,0:T(8,128)(2,1)S(1)}, bf16[256,512]{1,0:T(8,128)(2,1)S(1)}, u32[]{:S(2)}, u32[]{:S(2)}) collective-permute-start(bf16[256,512]{1,0:T(8,128)(2,1)S(1)} %get-tuple-element.21), channel_id=1, source_target_pairs={{0,6},{1,7},{2,0},{3,1},{4,2},{5,3},{6,4},{7,5},{8,14},{9,15},{10,... | collective-permute-start | bytes 786440 | tf_op jit(solution)/shard_map/ppermute | solution.py:18
  188.9 13.5 %collective-permute-start.21 = (bf16[256,512]{1,0:T(8,128)(2,1)S(1)}, bf16[256,512]{1,0:T(8,128)(2,1)S(1)}, u32[]{:S(2)}, u32[]{:S(2)}) collective-permute-start(bf16[256,512]{1,0:T(8,128)(2,1)S(1)} %get-tuple-element.22), channel_id=1, source_target_pairs={{0,4},{1,5},{2,6},{3,7},{4,0},{5,1},{6,2},{7,3},{8,12},{9,13},{10,... | collective-permute-start | bytes 786440 | tf_op jit(solution)/shard_map/ppermute | solution.py:18
  189.9 15.9 %collective-permute-start.11 = (bf16[256,512]{1,0:T(8,128)(2,1)S(1)}, bf16[256,512]{1,0:T(8,128)(2,1)S(1)}, u32[]{:S(2)}, u32[]{:S(2)}) collective-permute-start(bf16[256,512]{1,0:T(8,128)(2,1)S(1)} %add_convert_fusion.2), channel_id=1, source_target_pairs={{0,2},{1,3},{2,4},{3,5},{4,6},{5,7},{6,0},{7,1},{8,10},{9,11},{10,... | collective-permute-start | bytes 786440 | tf_op jit(solution)/shard_map/ppermute | solution.py:18
  191.3 21.3 %collective-permute-start.10 = (bf16[256,512]{1,0:T(8,128)(2,1)S(1)}, bf16[256,512]{1,0:T(8,128)(2,1)S(1)}, u32[]{:S(2)}, u32[]{:S(2)}) collective-permute-start(bf16[256,512]{1,0:T(8,128)(2,1)S(1)} %add_convert_fusion.2), channel_id=1, source_target_pairs={{0,4},{1,5},{2,6},{3,7},{4,0},{5,1},{6,2},{7,3},{8,12},{9,13},{10,... | collective-permute-start | bytes 786440 | tf_op jit(solution)/shard_map/ppermute | solution.py:18
  200.7 12.0 %collective-permute-start.9 = (bf16[256,512]{1,0:T(8,128)(2,1)S(1)}, bf16[256,512]{1,0:T(8,128)(2,1)S(1)}, u32[]{:S(2)}, u32[]{:S(2)}) collective-permute-start(bf16[256,512]{1,0:T(8,128)(2,1)S(1)} %add_convert_fusion.2), channel_id=1, source_target_pairs={{0,6},{1,7},{2,0},{3,1},{4,2},{5,3},{6,4},{7,5},{8,14},{9,15},{10,... | collective-permute-start | bytes 786440 | tf_op jit(solution)/shard_map/ppermute | solution.py:18
  202.5 24.9 %collective-permute-start.23 = (bf16[256,512]{1,0:T(8,128)(2,1)S(1)}, bf16[256,512]{1,0:T(8,128)(2,1)}, u32[]{:S(2)}, u32[]{:S(2)}) collective-permute-start(bf16[256,512]{1,0:T(8,128)(2,1)S(1)} %add_convert_fusion.1), channel_id=1, source_target_pairs={{0,1},{1,0},{2,3},{3,2},{4,5},{5,4},{6,7},{7,6},{8,9},{9,8},{10,11... | collective-permute-start | bytes 786440 | tf_op jit(solution)/shard_map/ppermute | solution.py:22
  222.9 9.6 %collective-permute-start.12 = (bf16[256,512]{1,0:T(8,128)(2,1)}, bf16[256,512]{1,0:T(8,128)(2,1)S(1)}, u32[]{:S(2)}, u32[]{:S(2)}) collective-permute-start(bf16[256,512]{1,0:T(8,128)(2,1)} %get-tuple-element.23), channel_id=1, source_target_pairs={{0,2},{1,3},{2,4},{3,5},{4,6},{5,7},{6,0},{7,1},{8,10},{9,11},{10,... | collective-permute-start | bytes 786440 | tf_op jit(solution)/shard_map/ppermute | solution.py:18
  223.4 16.1 %collective-permute-start.13 = (bf16[256,512]{1,0:T(8,128)(2,1)}, bf16[256,512]{1,0:T(8,128)(2,1)}, u32[]{:S(2)}, u32[]{:S(2)}) collective-permute-start(bf16[256,512]{1,0:T(8,128)(2,1)} %get-tuple-element.24), channel_id=1, source_target_pairs={{0,4},{1,5},{2,6},{3,7},{4,0},{5,1},{6,2},{7,3},{8,12},{9,13},{10,... | collective-permute-start | bytes 786440 | tf_op jit(solution)/shard_map/ppermute | solution.py:18
  226.4 13.8 %collective-permute-start.14 = (bf16[256,512]{1,0:T(8,128)(2,1)S(1)}, bf16[256,512]{1,0:T(8,128)(2,1)}, u32[]{:S(2)}, u32[]{:S(2)}) collective-permute-start(bf16[256,512]{1,0:T(8,128)(2,1)S(1)} %get-tuple-element.25), channel_id=1, source_target_pairs={{0,6},{1,7},{2,0},{3,1},{4,2},{5,3},{6,4},{7,5},{8,14},{9,15},{10,... | collective-permute-start | bytes 786440 | tf_op jit(solution)/shard_map/ppermute | solution.py:18
  228.5 14.5 %collective-permute-start.26 = (bf16[256,512]{1,0:T(8,128)(2,1)S(1)}, bf16[256,512]{1,0:T(8,128)(2,1)S(1)}, u32[]{:S(2)}, u32[]{:S(2)}) collective-permute-start(bf16[256,512]{1,0:T(8,128)(2,1)S(1)} %add_convert_fusion), channel_id=1, source_target_pairs={{0,2},{1,3},{2,4},{3,5},{4,6},{5,7},{6,0},{7,1},{8,10},{9,11},{10,... | collective-permute-start | bytes 786440 | tf_op jit(solution)/shard_map/ppermute | solution.py:18
  229.8 20.0 %collective-permute-start.25 = (bf16[256,512]{1,0:T(8,128)(2,1)S(1)}, bf16[256,512]{1,0:T(8,128)(2,1)S(1)}, u32[]{:S(2)}, u32[]{:S(2)}) collective-permute-start(bf16[256,512]{1,0:T(8,128)(2,1)S(1)} %add_convert_fusion), channel_id=1, source_target_pairs={{0,4},{1,5},{2,6},{3,7},{4,0},{5,1},{6,2},{7,3},{8,12},{9,13},{10,... | collective-permute-start | bytes 786440 | tf_op jit(solution)/shard_map/ppermute | solution.py:18
  232.5 17.3 %collective-permute-start.24 = (bf16[256,512]{1,0:T(8,128)(2,1)S(1)}, bf16[256,512]{1,0:T(8,128)(2,1)}, u32[]{:S(2)}, u32[]{:S(2)}) collective-permute-start(bf16[256,512]{1,0:T(8,128)(2,1)S(1)} %add_convert_fusion), channel_id=1, source_target_pairs={{0,6},{1,7},{2,0},{3,1},{4,2},{5,3},{6,4},{7,5},{8,14},{9,15},{10,... | collective-permute-start | bytes 786440 | tf_op jit(solution)/shard_map/ppermute | solution.py:18
  261.1 8.9 %collective-permute-start.27 = (bf16[256,512]{1,0:T(8,128)(2,1)}, bf16[256,512]{1,0:T(8,128)(2,1)S(1)}, u32[]{:S(2)}, u32[]{:S(2)}) collective-permute-start(bf16[256,512]{1,0:T(8,128)(2,1)} %get-tuple-element.17), channel_id=1, source_target_pairs={{0,2},{1,3},{2,4},{3,5},{4,6},{5,7},{6,0},{7,1},{8,10},{9,11},{10,... | collective-permute-start | bytes 786440 | tf_op jit(solution)/shard_map/ppermute | solution.py:18
  261.5 13.5 %collective-permute-start.29 = (bf16[256,512]{1,0:T(8,128)(2,1)}, bf16[256,512]{1,0:T(8,128)(2,1)S(1)}, u32[]{:S(2)}, u32[]{:S(2)}) collective-permute-start(bf16[256,512]{1,0:T(8,128)(2,1)} %get-tuple-element.18), channel_id=1, source_target_pairs={{0,6},{1,7},{2,0},{3,1},{4,2},{5,3},{6,4},{7,5},{8,14},{9,15},{10,... | collective-permute-start | bytes 786440 | tf_op jit(solution)/shard_map/ppermute | solution.py:18
  264.3 12.6 %collective-permute-start.28 = (bf16[256,512]{1,0:T(8,128)(2,1)S(1)}, bf16[256,512]{1,0:T(8,128)(2,1)}, u32[]{:S(2)}, u32[]{:S(2)}) collective-permute-start(bf16[256,512]{1,0:T(8,128)(2,1)S(1)} %get-tuple-element.19), channel_id=1, source_target_pairs={{0,4},{1,5},{2,6},{3,7},{4,0},{5,1},{6,2},{7,3},{8,12},{9,13},{10,... | collective-permute-start | bytes 786440 | tf_op jit(solution)/shard_map/ppermute | solution.py:18
  265.8 13.9 %collective-permute-start.15 = (bf16[256,256]{1,0:T(8,128)(2,1)}, bf16[256,256]{1,0:T(8,128)(2,1)S(1)}, u32[]{:S(2)}, u32[]{:S(2)}) collective-permute-start(bf16[256,256]{1,0:T(8,128)(2,1)} %fusion.57), channel_id=1, source_target_pairs={{0,1},{1,0},{2,3},{3,2},{4,5},{5,4},{6,7},{7,6},{8,9},{9,8},{10,11... | collective-permute-start | bytes 393224 | tf_op jit(solution)/shard_map/ppermute | solution.py:22
  278.5 9.0 %collective-permute-start.30 = (bf16[256,256]{1,0:T(8,128)(2,1)S(1)}, bf16[256,256]{1,0:T(8,128)(2,1)S(1)}, u32[]{:S(2)}, u32[]{:S(2)}) collective-permute-start(bf16[256,256]{1,0:T(8,128)(2,1)S(1)} %fusion.58), channel_id=1, source_target_pairs={{0,1},{1,0},{2,3},{3,2},{4,5},{5,4},{6,7},{7,6},{8,9},{9,8},{10,11... | collective-permute-start | bytes 393224 | tf_op jit(solution)/shard_map/ppermute | solution.py:22
  (21 other events, 409.4 us)
Sparse Core Ops, SparseCore 0:
  9.9 70.5 all-gather.1
